TPU v7x, 32 devices: a whole 2x2x4 slice. The times are simulated.
32 devices in a mesh: leaf: 8 (over z, y), case: 4 (over x, core).
Axes of the slice: x: 2, y: 2, z: 4, core: 2. Of those that a mesh axis runs over, the one named last changes fastest.
Arguments:
- features: bfloat16 [8, 16384, 128], P('case', 'leaf'), may hold values from -6 to 6
- cotangent: bfloat16 [8, 16384, 128], P('case', 'leaf'), may hold values from -6 to 6
- kernel_blocks: bfloat16 [128, 12, 128, 128], P('leaf'), may hold values from -0.15625 to 0.15625
- near_pairs: int32 [128, 12], P('leaf'), may hold values from 0 to 127, as said below
- leaf_basis: bfloat16 [64, 16384], P(None, 'leaf'), may hold values from -0.125 to 0.125
- w_near: bfloat16 [128, 128], replicated, may hold values from -0.5 to 0.5
- w_far: bfloat16 [128, 128], replicated, may hold values from -0.5 to 0.5
- translations: float32 [3, 64, 64], replicated, may hold values from -0.75 to 0.75
Outputs:
- output: bfloat16 [8, 16384, 128], P('case', 'leaf')
- grad_features: bfloat16 [8, 16384, 128], P('case', 'leaf')
- grad_near: float32 [128, 128], replicated
- grad_far: float32 [128, 128], replicated
Inputs may be any that keep to these rules, and one draw needn't show every extreme that they name: `near_pairs`: A target block held by one index of leaf names blocks of that index, or blocks at most 8 places beyond its first or last block; on every index both of these farthest blocks occur where they exist; 0 and 127 both occur.
All inputs are finite; a program needn't handle non-finite values.
Results may differ from a plain program's by a relative error of at most 0.0085.
Values may be sent and summed in bfloat16 or wider, within the bound.
No kernel may reach another device: no remote copies, remote signals or barrier semaphores. Data moves between devices by JAX's collectives and lax.ppermute only.
A program may use at most 128 MiB of HBM per device.

v0:
```python
import math
import jax
import jax.numpy as jnp
from jax import lax
from jax.sharding import PartitionSpec as P


def partner(shard, axis, apart):
    return lax.ppermute(shard, axis, [(i, i ^ 1 << apart) for i in range(lax.axis_size(axis))])


def with_halo(cells, sides, width):
    for axis, dim in sides:
        count = lax.axis_size(axis)
        ends = count - 1
        head = lax.slice_in_dim(cells, 0, width, axis=dim)
        tail = lax.slice_in_dim(cells, cells.shape[dim] - width, cells.shape[dim], axis=dim)
        cells = jnp.concatenate(
            [
                lax.ppermute(tail, axis, [(i, (i + 1) % count) for i in range(ends)]),
                cells,
                lax.ppermute(head, axis, [((i + 1) % count, i) for i in range(ends)]),
            ],
            axis=dim,
        )
    return cells


def shifted(value, axis, steps):
    count = lax.axis_size(axis)
    leading, last = (max(0, -steps), min(count, count - steps))
    return lax.ppermute(value, axis, [(source, source + steps) for source in range(leading, last)])


def apply_level(matrix, sibling, flipped):
    if flipped:
        return jnp.einsum("sr,asc->arc", matrix, sibling, precision=lax.Precision.HIGHEST)
    return jnp.einsum("rs,asc->arc", matrix, sibling, precision=lax.Precision.HIGHEST)


def expand(own_value, translations, flipped):
    depth_count = lax.axis_size("leaf").bit_length() - 1
    summed = jnp.zeros(own_value.shape, jnp.float32)
    node_value = own_value
    for height in range(depth_count):
        sibling = partner(node_value, "leaf", height)
        summed = summed + apply_level(translations[height], sibling, flipped)
        node_value = node_value + sibling
    return summed


def on_device(
    features, cotangent, kernel_blocks, near_pairs, leaf_basis, w_near, w_far, translations
):
    cases_here, points_here, width = features.shape
    blocks_here, pair_count, block_rows = (
        kernel_blocks.shape[0],
        kernel_blocks.shape[1],
        kernel_blocks.shape[2],
    )
    position = lax.axis_index("leaf")
    extended = with_halo(features, (("leaf", 1),), points_here)
    span_blocks = blocks_here + 2 * blocks_here
    ext_blocks = extended.reshape(cases_here, span_blocks, block_rows, width)
    local_ids = (near_pairs - (position * blocks_here - blocks_here)).reshape(-1)
    picked = jnp.take(ext_blocks, local_ids, axis=1).reshape(
        cases_here, blocks_here, pair_count, block_rows, width
    )
    near_sum = jnp.einsum(
        "bkij,abkjc->abic", kernel_blocks, picked, preferred_element_type=jnp.float32
    )
    near_bf = near_sum.reshape(cases_here, points_here, width).astype(jnp.bfloat16)
    summary = jnp.einsum("rp,apc->arc", leaf_basis, features, preferred_element_type=jnp.float32)
    expansion = expand(summary, translations, False)
    exp_bf = expansion.astype(jnp.bfloat16)
    far_coeff = jnp.einsum("arc,cd->ard", exp_bf, w_far, preferred_element_type=jnp.float32).astype(
        jnp.bfloat16
    )
    far_field = jnp.einsum("rp,ard->apd", leaf_basis, far_coeff, preferred_element_type=jnp.float32)
    mixed = (
        jnp.einsum("apc,cd->apd", near_bf, w_near, preferred_element_type=jnp.float32) + far_field
    )
    output = jax.nn.gelu(mixed).astype(jnp.bfloat16)
    _, pullback = jax.vjp(jax.nn.gelu, mixed)
    slope = pullback(cotangent.astype(jnp.float32))[0].astype(jnp.bfloat16)
    projected = jnp.einsum(
        "rp,apc->arc", leaf_basis, slope, preferred_element_type=jnp.float32
    ).astype(jnp.bfloat16)
    back_coeff = jnp.einsum("arc,dc->ard", projected, w_far, preferred_element_type=jnp.float32)
    back_exp = expand(back_coeff, translations, True)
    back_far = jnp.einsum(
        "rp,arc->apc", leaf_basis, back_exp.astype(jnp.bfloat16), preferred_element_type=jnp.float32
    )
    back_near = jnp.einsum("apc,dc->apd", slope, w_near, preferred_element_type=jnp.float32).astype(
        jnp.bfloat16
    )
    back_blocks = back_near.reshape(cases_here, blocks_here, block_rows, width)
    contrib = jnp.einsum(
        "bkij,abic->bkajc", kernel_blocks, back_blocks, preferred_element_type=jnp.float32
    )
    contrib = contrib.reshape(blocks_here * pair_count, cases_here, block_rows, width)
    landed = jax.ops.segment_sum(contrib, local_ids, num_segments=span_blocks)
    left_part = landed[:blocks_here]
    middle_part = landed[blocks_here : blocks_here + blocks_here]
    right_part = landed[blocks_here + blocks_here :]
    from_next = shifted(left_part.astype(jnp.bfloat16), "leaf", -1).astype(left_part.dtype)
    from_prev = shifted(right_part.astype(jnp.bfloat16), "leaf", 1).astype(right_part.dtype)
    gathered_near = middle_part + from_next + from_prev
    back_near_sum = gathered_near.transpose(1, 0, 2, 3).reshape(cases_here, points_here, width)
    grad_features = (back_near_sum + back_far).astype(jnp.bfloat16)
    scale = 1.0 / math.sqrt(
        cases_here * lax.axis_size("case") * points_here * lax.axis_size("leaf")
    )
    near_term = (
        jnp.einsum("apc,apd->cd", near_bf, slope, preferred_element_type=jnp.float32) * scale
    )
    far_term = (
        jnp.einsum("arc,ard->cd", exp_bf, projected, preferred_element_type=jnp.float32) * scale
    )
    grad_near, grad_far = lax.psum((near_term, far_term), ("leaf", "case"))
    return (output, grad_features, grad_near, grad_far)


def solution(mesh):
    return jax.shard_map(
        on_device,
        mesh=mesh,
        in_specs=(
            P("case", "leaf", None),
            P("case", "leaf", None),
            P("leaf", None, None, None),
            P("leaf", None),
            P(None, "leaf"),
            P(),
            P(),
            P(),
        ),
        out_specs=(P("case", "leaf", None), P("case", "leaf", None), P(), P()),
        check_vma=False,
    )
```

profile of v0, /device:TPU:0, one launch (start us, length us, event | category | flops | bytes accessed | tf_op | source)
XLA Modules:
  0.0 359.6 jit_solution(16556230183017255712)
XLA Ops:
  7.2 5.1 %collective-permute-start = (bf16[2,2048,128]{2,1,0:T(8,128)(2,1)}, bf16[2,2048,128]{2,1,0:T(8,128)(2,1)S(1)}, u32[]{:S(2)}, u32[]{:S(2)}) collective-permute-start(bf16[2,2048,128]{2,1,0:T(8,128)(2,1)} %param.8), channel_id=1, source_target_pairs={{0,4},{4,8},{8,12},{12,16},{16,20},{20,24},{24,28},{1,5},{5,9},{9,... | collective-permute-start | bytes 3145736 | tf_op jit(solution)/shard_map/ppermute | solution.py:20
  15.2 2.7 collective-permute-start.2
  18.8 39.9 %collective-permute-done.2 = f32[2,64,128]{2,1,0:T(8,128)S(1)} collective-permute-done((f32[2,64,128]{2,1,0:T(8,128)S(1)}, f32[2,64,128]{2,1,0:T(8,128)S(1)}, u32[]{:S(2)}, u32[]{:S(2)}) %collective-permute-start.2) | collective-permute-done | bytes 65568 | tf_op jit(solution)/shard_map/ppermute | solution.py:9
  58.7 3.5 collective-permute-start.3
  62.3 2.3 collective-permute-done.3
  64.5 3.1 collective-permute-start.4
  74.0 8.2 %gather_fusion = bf16[192,2,128,128]{3,2,1,0:T(8,128)(2,1)} fusion(bf16[2,48,128,128]{3,2,1,0:T(8,128)(2,1)S(1)} %bitcast.123, s32[1024]{0:T(1024)S(1)} %pad_clamp_fusion), kind=kCustom, calls=%fused_computation | custom fusion | bytes 25166592 | tf_op jit(solution)/shard_map/jit(_take)/gather | solution.py:66
  82.2 6.5 %copy.24 = bf16[2,192,128,128]{3,2,1,0:T(8,128)(2,1)S(1)} copy(bf16[2,192,128,128]{3,2,0,1:T(8,128)(2,1)} %bitcast.124) | data formatting | bytes 25165824 | tf_op jit(solution)/shard_map/jit(_take)/gather | solution.py:66
  88.7 5.5 %fusion.21 = bf16[2,16,128,128]{3,2,0,1:T(8,128)(2,1)} fusion(bf16[16,12,128,128]{3,2,1,0:T(8,128)(2,1)} %param.10, bf16[2,16,12,128,128]{4,3,2,1,0:T(8,128)(2,1)S(1)} %bitcast.125, pred[16,12]{1,0:T(8,128)(4,1)S(1)} %get-tuple-element.18), kind=kOutput, calls=%fused_computation.33 | convolution fusion | flops 1617428480 | bytes 19923136 | tf_op jit(solution)/shard_map/bkij,abkjc->abic/dot_general | solution.py:69
  97.3 5.0 %fusion.7 = (bf16[2,2048,128]{2,1,0:T(8,128)(2,1)S(1)}, bf16[2,2048,128]{2,1,0:T(8,128)(2,1)}) fusion(bf16[2,2048,128]{2,1,0:T(8,128)(2,1)} %param.9, f32[2,2048,128]{2,1,0:T(8,128)} %fusion.55, bf16[64,2048]{1,0:T(8,128)(2,1)S(1)} %copy-done, bf16[2,64,128]{2,1,0:T(8,128)(2,1)S(1)} %fusion.34, bf16[128,128]{1,0:T(8,128)(2,1)S(1)} %copy-done.8), kind=kOutput, calls=%fused_computation.19 | convolution fusion | flops 83902464 | bytes 5570560 | tf_op jit(solution)/shard_map/rp,ard->apd/dot_general | solution.py:79
  104.8 12.9 %convolution_bitcast_fusion = f32[16,12,2,128,128]{3,4,1,2,0:T(8,128)} fusion(bf16[16,12,128,128]{3,2,1,0:T(8,128)(2,1)} %param.10, bf16[2,16,128,128,1]{3,2,1,0,4:T(8,128)(2,1)S(1)} %bitcast.128), kind=kOutput, calls=%fused_computation.5 | convolution fusion | flops 1610612736 | bytes 32505856 | tf_op jit(solution)/shard_map/bkij,abic->bkajc/dot_general | solution.py:98
  117.7 24.7 %copy.29 = f32[16,12,2,128,128]{4,3,2,1,0:T(8,128)} copy(f32[16,12,2,128,128]{3,4,1,2,0:T(8,128)} %convolution_bitcast_fusion) | data formatting | bytes 50331648 | tf_op jit(solution)/shard_map/bkij,abic->bkajc/transpose | solution.py:98
  142.4 3.5 broadcast_in_dim.15
  145.9 56.4 %scatter_fusion = f32[48,2,128,128]{3,2,1,0:T(8,128)} fusion(f32[48,2,128,128]{3,2,1,0:T(8,128)} %broadcast_in_dim.15, s32[192]{0:T(256)S(1)} %reshape.77, f32[192,2,128,128]{3,2,1,0:T(8,128)} %bitcast.122), kind=kCustom, calls=%fused_computation.1 | custom fusion | flops 6291456 | bytes 75498240 | tf_op jit(solution)/shard_map/scatter-add | solution.py:102
  202.3 3.5 convert.4
  209.3 5.5 %collective-permute-start.6 = (bf16[16,2,128,128]{3,2,1,0:T(8,128)(2,1)S(1)}, bf16[16,2,128,128]{3,2,1,0:T(8,128)(2,1)}, u32[]{:S(2)}, u32[]{:S(2)}) collective-permute-start(bf16[16,2,128,128]{3,2,1,0:T(8,128)(2,1)S(1)} %get-tuple-element.21), channel_id=1, source_target_pairs={{0,4},{4,8},{8,12},{12,16},{16,20},{20,24},{24,28},{1,5},{5,9},{9,... | collective-permute-start | bytes 3145736 | tf_op jit(solution)/shard_map/ppermute | solution.py:32
  217.6 17.8 %collective-permute-done.8 = f32[2,64,128]{2,1,0:T(8,128)S(1)} collective-permute-done((f32[2,64,128]{2,1,0:T(8,128)S(1)}, f32[2,64,128]{2,1,0:T(8,128)S(1)}, u32[]{:S(2)}, u32[]{:S(2)}) %collective-permute-start.8) | collective-permute-done | bytes 65568 | tf_op jit(solution)/shard_map/ppermute | solution.py:9
  235.4 3.8 %collective-permute-start.9 = (f32[2,64,128]{2,1,0:T(8,128)S(1)}, f32[2,64,128]{2,1,0:T(8,128)S(1)}, u32[]{:S(2)}, u32[]{:S(2)}) collective-permute-start(f32[2,64,128]{2,1,0:T(8,128)S(1)} %add.93), channel_id=1, source_target_pairs={{0,16},{4,20},{8,24},{12,28},{16,0},{20,4},{24,8},{28,12},{1,17},{... | collective-permute-start | bytes 196616 | tf_op jit(solution)/shard_map/ppermute | solution.py:9
  239.5 2.0 collective-permute-done.9
  245.6 9.9 %collective-permute-done.6 = bf16[16,2,128,128]{3,2,1,0:T(8,128)(2,1)} collective-permute-done((bf16[16,2,128,128]{3,2,1,0:T(8,128)(2,1)S(1)}, bf16[16,2,128,128]{3,2,1,0:T(8,128)(2,1)}, u32[]{:S(2)}, u32[]{:S(2)}) %collective-permute-start.6) | collective-permute-done | bytes 1048608 | tf_op jit(solution)/shard_map/ppermute | solution.py:32
  255.5 2.6 fusion.16
  258.1 2.0 copy.30
  260.1 2.8 reshape.66
  266.1 83.7 %all-reduce.3.cloned.1.call-done = (f32[128,128]{1,0:T(8,128)}, f32[128,128]{1,0:T(8,128)}) async-done(((f32[128,128]{1,0:T(8,128)}, f32[128,128]{1,0:T(8,128)}), (f32[128,128]{1,0:T(8,128)}, f32[128,128]{1,0:T(8,128)})) %all-reduce.3.cloned.1.call-update) | async-done | bytes 131088 | tf_op jit(solution)/shard_map/psum | solution.py:120
  (59 shorter events, 32.3 us)
Async XLA Ops:
  7.2 6.5 %copy-start = (bf16[64,2048]{1,0:T(8,128)(2,1)S(1)}, bf16[64,2048]{1,0:T(8,128)(2,1)}, u32[]{:S(2)}) copy-start(bf16[64,2048]{1,0:T(8,128)(2,1)} %param.12) | copy-start | bytes 786436
  7.2 63.6 %copy-start.4 = (f32[3,64,64]{2,1,0:T(8,128)S(1)}, f32[3,64,64]{2,1,0:T(8,128)}, u32[]{:S(2)}) copy-start(f32[3,64,64]{2,1,0:T(8,128)} %param.15) | copy-start | bytes 147460
  7.2 342.6 %all-reduce.3.cloned.1.call-start = ((), (), s32[]{:S(2)}) async-start(), calls=%async_computation | async-start | bytes 262144 | tf_op jit(solution)/shard_map/psum | solution.py:120
  7.2 63.8 %collective-permute-start = (bf16[2,2048,128]{2,1,0:T(8,128)(2,1)}, bf16[2,2048,128]{2,1,0:T(8,128)(2,1)S(1)}, u32[]{:S(2)}, u32[]{:S(2)}) collective-permute-start(bf16[2,2048,128]{2,1,0:T(8,128)(2,1)} %param.8), channel_id=1, source_target_pairs={{0,4},{4,8},{8,12},{12,16},{16,20},{20,24},{24,28},{1,5},{5,9},{9,... | collective-permute-start | bytes 3145736 | tf_op jit(solution)/shard_map/ppermute | solution.py:20
  12.3 59.7 %collective-permute-start.1 = (bf16[2,2048,128]{2,1,0:T(8,128)(2,1)}, bf16[2,2048,128]{2,1,0:T(8,128)(2,1)}, u32[]{:S(2)}, u32[]{:S(2)}) collective-permute-start(bf16[2,2048,128]{2,1,0:T(8,128)(2,1)} %param.8), channel_id=1, source_target_pairs={{4,0},{8,4},{12,8},{16,12},{20,16},{24,20},{28,24},{5,1},{9,5},{13... | collective-permute-start | bytes 3145736 | tf_op jit(solution)/shard_map/ppermute | solution.py:22
  15.2 43.6 %collective-permute-start.2 = (f32[2,64,128]{2,1,0:T(8,128)S(1)}, f32[2,64,128]{2,1,0:T(8,128)S(1)}, u32[]{:S(2)}, u32[]{:S(2)}) collective-permute-start(f32[2,64,128]{2,1,0:T(8,128)S(1)} %convolution_bitcast_fusion.3), channel_id=1, source_target_pairs={{0,4},{4,0},{8,12},{12,8},{16,20},{20,16},{24,28},{28,24},{1,5},{5... | collective-permute-start | bytes 196616 | tf_op jit(solution)/shard_map/ppermute | solution.py:9
  58.7 5.8 %collective-permute-start.3 = (f32[2,64,128]{2,1,0:T(8,128)S(1)}, f32[2,64,128]{2,1,0:T(8,128)S(1)}, u32[]{:S(2)}, u32[]{:S(2)}) collective-permute-start(f32[2,64,128]{2,1,0:T(8,128)S(1)} %add.82), channel_id=1, source_target_pairs={{0,8},{4,12},{8,0},{12,4},{16,24},{20,28},{24,16},{28,20},{1,9},{5... | collective-permute-start | bytes 196616 | tf_op jit(solution)/shard_map/ppermute | solution.py:9
  64.5 5.3 %collective-permute-start.4 = (f32[2,64,128]{2,1,0:T(8,128)S(1)}, f32[2,64,128]{2,1,0:T(8,128)S(1)}, u32[]{:S(2)}, u32[]{:S(2)}) collective-permute-start(f32[2,64,128]{2,1,0:T(8,128)S(1)} %add.84), channel_id=1, source_target_pairs={{0,16},{4,20},{8,24},{12,28},{16,0},{20,4},{24,8},{28,12},{1,17},{... | collective-permute-start | bytes 196616 | tf_op jit(solution)/shard_map/ppermute | solution.py:9
  71.0 26.3 %copy-start.6 = (bf16[2,64,128]{2,1,0:T(8,128)(2,1)}, bf16[2,64,128]{2,1,0:T(8,128)(2,1)S(1)}, u32[]{:S(2)}) copy-start(bf16[2,64,128]{2,1,0:T(8,128)(2,1)S(1)} %fusion.34) | copy-start | bytes 98308
  71.1 1.0 copy-start.2
  94.2 1.3 copy-start.5
  95.5 1.8 copy-start.8
  103.8 111.0 %collective-permute-start.7 = (f32[2,64,128]{2,1,0:T(8,128)}, f32[2,64,128]{2,1,0:T(8,128)}, u32[]{:S(2)}, u32[]{:S(2)}) collective-permute-start(f32[2,64,128]{2,1,0:T(8,128)} %fusion.40), channel_id=1, source_target_pairs={{0,4},{4,0},{8,12},{12,8},{16,20},{20,16},{24,28},{28,24},{1,5},{5... | collective-permute-start | bytes 196616 | tf_op jit(solution)/shard_map/ppermute | solution.py:9
  206.9 9.9 %copy-start.7 = (bf16[2,64,128]{2,1,0:T(8,128)(2,1)S(1)}, bf16[2,64,128]{2,1,0:T(8,128)(2,1)}, u32[]{:S(2)}) copy-start(bf16[2,64,128]{2,1,0:T(8,128)(2,1)} %copy-done.6) | copy-start | bytes 98308
  208.0 36.6 %collective-permute-start.5 = (bf16[16,2,128,128]{3,2,1,0:T(8,128)(2,1)}, bf16[16,2,128,128]{3,2,1,0:T(8,128)(2,1)S(1)}, u32[]{:S(2)}, u32[]{:S(2)}) collective-permute-start(bf16[16,2,128,128]{3,2,1,0:T(8,128)(2,1)} %get-tuple-element.20), channel_id=1, source_target_pairs={{4,0},{8,4},{12,8},{16,12},{20,16},{24,20},{28,24},{5,1},{9,5},{13... | collective-permute-start | bytes 3145736 | tf_op jit(solution)/shard_map/ppermute | solution.py:32
  209.3 46.2 %collective-permute-start.6 = (bf16[16,2,128,128]{3,2,1,0:T(8,128)(2,1)S(1)}, bf16[16,2,128,128]{3,2,1,0:T(8,128)(2,1)}, u32[]{:S(2)}, u32[]{:S(2)}) collective-permute-start(bf16[16,2,128,128]{3,2,1,0:T(8,128)(2,1)S(1)} %get-tuple-element.21), channel_id=1, source_target_pairs={{0,4},{4,8},{8,12},{12,16},{16,20},{20,24},{24,28},{1,5},{5,9},{9,... | collective-permute-start | bytes 3145736 | tf_op jit(solution)/shard_map/ppermute | solution.py:32
  215.7 19.7 %collective-permute-start.8 = (f32[2,64,128]{2,1,0:T(8,128)S(1)}, f32[2,64,128]{2,1,0:T(8,128)S(1)}, u32[]{:S(2)}, u32[]{:S(2)}) collective-permute-start(f32[2,64,128]{2,1,0:T(8,128)S(1)} %add.91), channel_id=1, source_target_pairs={{0,8},{4,12},{8,0},{12,4},{16,24},{20,28},{24,16},{28,20},{1,9},{5... | collective-permute-start | bytes 196616 | tf_op jit(solution)/shard_map/ppermute | solution.py:9
  235.4 6.0 %collective-permute-start.9 = (f32[2,64,128]{2,1,0:T(8,128)S(1)}, f32[2,64,128]{2,1,0:T(8,128)S(1)}, u32[]{:S(2)}, u32[]{:S(2)}) collective-permute-start(f32[2,64,128]{2,1,0:T(8,128)S(1)} %add.93), channel_id=1, source_target_pairs={{0,16},{4,20},{8,24},{12,28},{16,0},{20,4},{24,8},{28,12},{1,17},{... | collective-permute-start | bytes 196616 | tf_op jit(solution)/shard_map/ppermute | solution.py:9
  244.6 1.0 copy-start.3
  260.1 2.8 copy-start.1
Sparse Core Ops, SparseCore 0:
  217.7 132.0 all-reduce.2
where the time goes:
time: 361 us; the launch traced here: 360 us
  waiting for transfers between devices  157 us (43%)
  other arithmetic  67.9 us (19%)
  local copies, waits for them, and re-layouts  56.5 us (16%)
  matrix products  35.6 us (10%)
  starting transfers between devices  28.3 us (8%)
  between operations  14.3 us (4%)
    psum x1, waiting for transfers between devices, on_device(): grad_near, grad_far = lax.psum((near_term, far_term), ('leaf', 'case'))  83.7 us
    ppermute x6, waiting for transfers between devices, partner(): lax.ppermute(shard, axis, [(i, i ^ 1 << apart) for i in range(lax.axis_si...  63.3 us
    scatter-add x1, other arithmetic, on_device(): landed = jax.ops.segment_sum(contrib, local_ids, num_segments=span_blocks)  56.4 us
    transpose x1, local copies, waits for them, and re-layouts, on_device(): jnp.einsum('bkij,abic->bkajc', kernel_blocks, back_blocks, preferred_elem...  24.7 us
    ppermute x6, starting transfers between devices, partner(): lax.ppermute(shard, axis, [(i, i ^ 1 << apart) for i in range(lax.axis_si...  15.1 us
    gather x2, local copies, waits for them, and re-layouts, on_device(): jnp.take(ext_blocks, local_ids, axis=1)  14.7 us
    dot_general x1, matrix products, on_device(): jnp.einsum('bkij,abic->bkajc', kernel_blocks, back_blocks, preferred_elem...  12.9 us
    ppermute x2, waiting for transfers between devices, shifted(): lax.ppermute(value, axis, [(source, source + steps) for source in range(l...  9.93 us
  transfers between devices with their start and end apart: 11, of which 7 were waited for; matrix products, arithmetic and copies ran while one was open for 34% of the time, Pallas kernels for 0%

commit v1 on v0

--- a/solution.py
+++ b/solution.py
@@ -3,6 +3,11 @@
 import jax.numpy as jnp
 from jax import lax
 from jax.sharding import PartitionSpec as P
+
+
+def by_each_axis(value_2, first, second):
+    inner = lax.psum(value_2, first)
+    return lax.psum(inner, second)
 
 
 def partner(shard, axis, apart):
@@ -117,7 +122,7 @@
     far_term = (
         jnp.einsum("arc,ard->cd", exp_bf, projected, preferred_element_type=jnp.float32) * scale
     )
-    grad_near, grad_far = lax.psum((near_term, far_term), ("leaf", "case"))
+    grad_near, grad_far = by_each_axis((near_term, far_term), "case", "leaf")
     return (output, grad_features, grad_near, grad_far)
 
 

time: 361 us -> 332 us (0.920)
  waiting for transfers between devices: 157 us -> 129 us
    ppermute x6, waiting for transfers between devices: 63.3 us -> 45.2 us  [partner(): lax.ppermute(shard, axis, [(i, i ^ 1 << apart) for i in range(lax.axis_si...]
    ppermute x2, waiting for transfers between devices: 9.93 us -> 0.01 us  [shifted(): lax.ppermute(value, axis, [(source, source + steps) for source in range(l...]
    psum x1 -> x2, waiting for transfers between devices: 83.7 us -> 84.2 us  [the longest x1 54.2 us: by_each_axis(): return lax.psum(inner, second)]
  transfers between devices with their start and end apart: 11 -> 12, of which waited for: 7 -> 6; matrix products, arithmetic and copies ran while one was open for 34% -> 37% of each run, Pallas kernels for 0% -> 0%
where the time goes in v1:
time: 332 us; the launch traced here: 331 us
  waiting for transfers between devices  129 us (39%)
  other arithmetic  69.2 us (21%)
  local copies, waits for them, and re-layouts  54.6 us (16%)
  matrix products  36.5 us (11%)
  starting transfers between devices  27.1 us (8%)
  between operations  14.3 us (4%)
    scatter-add x1, other arithmetic, on_device(): landed = jax.ops.segment_sum(contrib, local_ids, num_segments=span_blocks)  56.5 us
    psum x1, waiting for transfers between devices, by_each_axis(): return lax.psum(inner, second)  54.2 us
    ppermute x6, waiting for transfers between devices, partner(): lax.ppermute(shard, axis, [(i, i ^ 1 << apart) for i in range(lax.axis_si...  45.2 us
    psum x1, waiting for transfers between devices, by_each_axis(): inner = lax.psum(value_2, first)  30 us
    transpose x1, local copies, waits for them, and re-layouts, on_device(): jnp.einsum('bkij,abic->bkajc', kernel_blocks, back_blocks, preferred_elem...  24.7 us
    gather x2, local copies, waits for them, and re-layouts, on_device(): jnp.take(ext_blocks, local_ids, axis=1)  14.7 us
    ppermute x6, starting transfers between devices, partner(): lax.ppermute(shard, axis, [(i, i ^ 1 << apart) for i in range(lax.axis_si...  13.6 us
    dot_general x1, matrix products, on_device(): jnp.einsum('bkij,abic->bkajc', kernel_blocks, back_blocks, preferred_elem...  13 us
  transfers between devices with their start and end apart: 12, of which 6 were waited for; matrix products, arithmetic and copies ran while one was open for 37% of the time, Pallas kernels for 0%

profile of v1, /device:TPU:0, one launch (start us, length us, event | category | flops | bytes accessed | tf_op | source)
XLA Modules:
  0.0 331.0 jit_solution(9374910898323474554)
XLA Ops:
  7.2 5.1 %collective-permute-start = (bf16[2,2048,128]{2,1,0:T(8,128)(2,1)}, bf16[2,2048,128]{2,1,0:T(8,128)(2,1)S(1)}, u32[]{:S(2)}, u32[]{:S(2)}) collective-permute-start(bf16[2,2048,128]{2,1,0:T(8,128)(2,1)} %param.8), channel_id=1, source_target_pairs={{0,4},{4,8},{8,12},{12,16},{16,20},{20,24},{24,28},{1,5},{5,9},{9,... | collective-permute-start | bytes 3145736 | tf_op jit(solution)/shard_map/ppermute | solution.py:25
  15.2 2.7 collective-permute-start.2
  18.8 39.9 %collective-permute-done.2 = f32[2,64,128]{2,1,0:T(8,128)S(1)} collective-permute-done((f32[2,64,128]{2,1,0:T(8,128)S(1)}, f32[2,64,128]{2,1,0:T(8,128)S(1)}, u32[]{:S(2)}, u32[]{:S(2)}) %collective-permute-start.2) | collective-permute-done | bytes 65568 | tf_op jit(solution)/shard_map/ppermute | solution.py:14
  58.7 3.5 %collective-permute-start.3 = (f32[2,64,128]{2,1,0:T(8,128)S(1)}, f32[2,64,128]{2,1,0:T(8,128)S(1)}, u32[]{:S(2)}, u32[]{:S(2)}) collective-permute-start(f32[2,64,128]{2,1,0:T(8,128)S(1)} %add.86), channel_id=1, source_target_pairs={{0,8},{4,12},{8,0},{12,4},{16,24},{20,28},{24,16},{28,20},{1,9},{5... | collective-permute-start | bytes 196616 | tf_op jit(solution)/shard_map/ppermute | solution.py:14
  62.3 2.3 collective-permute-done.3
  64.5 3.1 collective-permute-start.4
  72.0 2.0 pad_maximum_fusion
  74.0 8.2 %gather_fusion = bf16[192,2,128,128]{3,2,1,0:T(8,128)(2,1)} fusion(bf16[2,48,128,128]{3,2,1,0:T(8,128)(2,1)S(1)} %bitcast.123, s32[1024]{0:T(1024)S(1)} %pad_clamp_fusion), kind=kCustom, calls=%fused_computation | custom fusion | bytes 25166592 | tf_op jit(solution)/shard_map/jit(_take)/gather | solution.py:71
  82.2 6.5 %copy.24 = bf16[2,192,128,128]{3,2,1,0:T(8,128)(2,1)S(1)} copy(bf16[2,192,128,128]{3,2,0,1:T(8,128)(2,1)} %bitcast.124) | data formatting | bytes 25165824 | tf_op jit(solution)/shard_map/jit(_take)/gather | solution.py:71
  88.7 5.5 %fusion.21 = bf16[2,16,128,128]{3,2,0,1:T(8,128)(2,1)} fusion(bf16[16,12,128,128]{3,2,1,0:T(8,128)(2,1)} %param.10, bf16[2,16,12,128,128]{4,3,2,1,0:T(8,128)(2,1)S(1)} %bitcast.125, pred[16,12]{1,0:T(8,128)(4,1)S(1)} %get-tuple-element.20), kind=kOutput, calls=%fused_computation.33 | convolution fusion | flops 1617428480 | bytes 19923136 | tf_op jit(solution)/shard_map/bkij,abkjc->abic/dot_general | solution.py:74
  97.3 5.0 %fusion.7 = (bf16[2,2048,128]{2,1,0:T(8,128)(2,1)S(1)}, bf16[2,2048,128]{2,1,0:T(8,128)(2,1)}) fusion(bf16[2,2048,128]{2,1,0:T(8,128)(2,1)} %param.9, f32[2,2048,128]{2,1,0:T(8,128)} %fusion.55, bf16[64,2048]{1,0:T(8,128)(2,1)S(1)} %copy-done, bf16[2,64,128]{2,1,0:T(8,128)(2,1)S(1)} %fusion.34, bf16[128,128]{1,0:T(8,128)(2,1)S(1)} %copy-done.7), kind=kOutput, calls=%fused_computation.19 | convolution fusion | flops 83902464 | bytes 5570560 | tf_op jit(solution)/shard_map/rp,ard->apd/dot_general | solution.py:84
  105.9 13.0 %convolution_bitcast_fusion = f32[16,12,2,128,128]{3,4,1,2,0:T(8,128)} fusion(bf16[16,12,128,128]{3,2,1,0:T(8,128)(2,1)} %param.10, bf16[2,16,128,128,1]{3,2,1,0,4:T(8,128)(2,1)S(1)} %bitcast.128), kind=kOutput, calls=%fused_computation.5 | convolution fusion | flops 1610612736 | bytes 32505856 | tf_op jit(solution)/shard_map/bkij,abic->bkajc/dot_general | solution.py:103
  118.9 24.7 %copy.29 = f32[16,12,2,128,128]{4,3,2,1,0:T(8,128)} copy(f32[16,12,2,128,128]{3,4,1,2,0:T(8,128)} %convolution_bitcast_fusion) | data formatting | bytes 50331648 | tf_op jit(solution)/shard_map/bkij,abic->bkajc/transpose | solution.py:103
  143.6 3.5 %broadcast_in_dim.15 = f32[48,2,128,128]{3,2,1,0:T(8,128)} broadcast(f32[]{:T(128)} %constant.38.clone.1), dimensions={} | broadcast | bytes 6291460 | tf_op jit(solution)/shard_map/broadcast_in_dim | solution.py:107
  147.0 56.5 %scatter_fusion = f32[48,2,128,128]{3,2,1,0:T(8,128)} fusion(f32[48,2,128,128]{3,2,1,0:T(8,128)} %broadcast_in_dim.15, s32[192]{0:T(256)S(1)} %reshape.77, f32[192,2,128,128]{3,2,1,0:T(8,128)} %bitcast.122), kind=kCustom, calls=%fused_computation.1 | custom fusion | flops 6291456 | bytes 75498240 | tf_op jit(solution)/shard_map/scatter-add | solution.py:107
  203.5 3.5 %convert.4 = bf16[48,2,128,128]{3,2,1,0:T(8,128)(2,1)S(1)} convert(f32[48,2,128,128]{3,2,1,0:T(8,128)} %scatter_fusion) | non-fusion elementwise | flops 1572864 | bytes 9437184 | tf_op jit(solution)/shard_map/convert.1
  208.5 5.5 %collective-permute-start.6 = (bf16[16,2,128,128]{3,2,1,0:T(8,128)(2,1)S(1)}, bf16[16,2,128,128]{3,2,1,0:T(8,128)(2,1)}, u32[]{:S(2)}, u32[]{:S(2)}) collective-permute-start(bf16[16,2,128,128]{3,2,1,0:T(8,128)(2,1)S(1)} %get-tuple-element.23), channel_id=1, source_target_pairs={{0,4},{4,8},{8,12},{12,16},{16,20},{20,24},{24,28},{1,5},{5,9},{9,... | collective-permute-start | bytes 3145736 | tf_op jit(solution)/shard_map/ppermute | solution.py:37
  217.5 30.0 %all-reduce.7.cloned.1.call-done = (f32[128,128]{1,0:T(8,128)}, f32[128,128]{1,0:T(8,128)}) async-done(((f32[128,128]{1,0:T(8,128)}, f32[128,128]{1,0:T(8,128)}), (f32[128,128]{1,0:T(8,128)}, f32[128,128]{1,0:T(8,128)})) %all-reduce.7.cloned.1.call-update) | async-done | bytes 131088 | tf_op jit(solution)/shard_map/psum | solution.py:9
  248.4 2.5 collective-permute-start.9
  256.7 2.3 fusion.16
  259.0 2.0 copy.30
  261.0 2.8 reshape.66
  263.9 1.8 add_convert_fusion
  267.0 54.2 %all-reduce.5.cloned.1.call-done = (f32[128,128]{1,0:T(8,128)}, f32[128,128]{1,0:T(8,128)}) async-done(((f32[128,128]{1,0:T(8,128)}, f32[128,128]{1,0:T(8,128)}), (f32[128,128]{1,0:T(8,128)}, f32[128,128]{1,0:T(8,128)})) %all-reduce.5.cloned.1.call-update) | async-done | bytes 131088 | tf_op jit(solution)/shard_map/psum | solution.py:10
  (60 shorter events, 30.7 us)
Async XLA Ops:
  7.2 6.5 %copy-start = (bf16[64,2048]{1,0:T(8,128)(2,1)S(1)}, bf16[64,2048]{1,0:T(8,128)(2,1)}, u32[]{:S(2)}) copy-start(bf16[64,2048]{1,0:T(8,128)(2,1)} %param.12) | copy-start | bytes 786436
  7.2 63.6 %copy-start.3 = (f32[3,64,64]{2,1,0:T(8,128)S(1)}, f32[3,64,64]{2,1,0:T(8,128)}, u32[]{:S(2)}) copy-start(f32[3,64,64]{2,1,0:T(8,128)} %param.15) | copy-start | bytes 147460
  7.2 240.2 %all-reduce.7.cloned.1.call-start = ((), (), s32[]{:S(2)}) async-start(), calls=%async_computation.1 | async-start | bytes 262144 | tf_op jit(solution)/shard_map/psum | solution.py:9
  7.2 63.8 %collective-permute-start = (bf16[2,2048,128]{2,1,0:T(8,128)(2,1)}, bf16[2,2048,128]{2,1,0:T(8,128)(2,1)S(1)}, u32[]{:S(2)}, u32[]{:S(2)}) collective-permute-start(bf16[2,2048,128]{2,1,0:T(8,128)(2,1)} %param.8), channel_id=1, source_target_pairs={{0,4},{4,8},{8,12},{12,16},{16,20},{20,24},{24,28},{1,5},{5,9},{9,... | collective-permute-start | bytes 3145736 | tf_op jit(solution)/shard_map/ppermute | solution.py:25
  12.3 59.7 %collective-permute-start.1 = (bf16[2,2048,128]{2,1,0:T(8,128)(2,1)}, bf16[2,2048,128]{2,1,0:T(8,128)(2,1)}, u32[]{:S(2)}, u32[]{:S(2)}) collective-permute-start(bf16[2,2048,128]{2,1,0:T(8,128)(2,1)} %param.8), channel_id=1, source_target_pairs={{4,0},{8,4},{12,8},{16,12},{20,16},{24,20},{28,24},{5,1},{9,5},{13... | collective-permute-start | bytes 3145736 | tf_op jit(solution)/shard_map/ppermute | solution.py:27
  15.2 43.6 %collective-permute-start.2 = (f32[2,64,128]{2,1,0:T(8,128)S(1)}, f32[2,64,128]{2,1,0:T(8,128)S(1)}, u32[]{:S(2)}, u32[]{:S(2)}) collective-permute-start(f32[2,64,128]{2,1,0:T(8,128)S(1)} %convolution_bitcast_fusion.3), channel_id=1, source_target_pairs={{0,4},{4,0},{8,12},{12,8},{16,20},{20,16},{24,28},{28,24},{1,5},{5... | collective-permute-start | bytes 196616 | tf_op jit(solution)/shard_map/ppermute | solution.py:14
  58.7 5.8 %collective-permute-start.3 = (f32[2,64,128]{2,1,0:T(8,128)S(1)}, f32[2,64,128]{2,1,0:T(8,128)S(1)}, u32[]{:S(2)}, u32[]{:S(2)}) collective-permute-start(f32[2,64,128]{2,1,0:T(8,128)S(1)} %add.86), channel_id=1, source_target_pairs={{0,8},{4,12},{8,0},{12,4},{16,24},{20,28},{24,16},{28,20},{1,9},{5... | collective-permute-start | bytes 196616 | tf_op jit(solution)/shard_map/ppermute | solution.py:14
  64.5 5.3 %collective-permute-start.4 = (f32[2,64,128]{2,1,0:T(8,128)S(1)}, f32[2,64,128]{2,1,0:T(8,128)S(1)}, u32[]{:S(2)}, u32[]{:S(2)}) collective-permute-start(f32[2,64,128]{2,1,0:T(8,128)S(1)} %add.88), channel_id=1, source_target_pairs={{0,16},{4,20},{8,24},{12,28},{16,0},{20,4},{24,8},{28,12},{1,17},{... | collective-permute-start | bytes 196616 | tf_op jit(solution)/shard_map/ppermute | solution.py:14
  71.0 26.3 %copy-start.5 = (bf16[2,64,128]{2,1,0:T(8,128)(2,1)}, bf16[2,64,128]{2,1,0:T(8,128)(2,1)S(1)}, u32[]{:S(2)}) copy-start(bf16[2,64,128]{2,1,0:T(8,128)(2,1)S(1)} %fusion.34) | copy-start | bytes 98308
  71.1 1.0 copy-start.2
  94.2 1.3 copy-start.4
  95.5 1.8 copy-start.7
  104.9 110.2 %collective-permute-start.7 = (f32[2,64,128]{2,1,0:T(8,128)}, f32[2,64,128]{2,1,0:T(8,128)}, u32[]{:S(2)}, u32[]{:S(2)}) collective-permute-start(f32[2,64,128]{2,1,0:T(8,128)} %fusion.40), channel_id=1, source_target_pairs={{0,4},{4,0},{8,12},{12,8},{16,20},{20,16},{24,28},{28,24},{1,5},{5... | collective-permute-start | bytes 196616 | tf_op jit(solution)/shard_map/ppermute | solution.py:14
  207.0 7.0 %copy-start.6 = (bf16[2,64,128]{2,1,0:T(8,128)(2,1)S(1)}, bf16[2,64,128]{2,1,0:T(8,128)(2,1)}, u32[]{:S(2)}) copy-start(bf16[2,64,128]{2,1,0:T(8,128)(2,1)} %copy-done.5) | copy-start | bytes 98308
  207.2 49.6 %collective-permute-start.5 = (bf16[16,2,128,128]{3,2,1,0:T(8,128)(2,1)S(1)}, bf16[16,2,128,128]{3,2,1,0:T(8,128)(2,1)S(1)}, u32[]{:S(2)}, u32[]{:S(2)}) collective-permute-start(bf16[16,2,128,128]{3,2,1,0:T(8,128)(2,1)S(1)} %get-tuple-element.22), channel_id=1, source_target_pairs={{4,0},{8,4},{12,8},{16,12},{20,16},{24,20},{28,24},{5,1},{9,5},{13... | collective-permute-start | bytes 3145736 | tf_op jit(solution)/shard_map/ppermute | solution.py:37
  208.5 48.3 %collective-permute-start.6 = (bf16[16,2,128,128]{3,2,1,0:T(8,128)(2,1)S(1)}, bf16[16,2,128,128]{3,2,1,0:T(8,128)(2,1)}, u32[]{:S(2)}, u32[]{:S(2)}) collective-permute-start(bf16[16,2,128,128]{3,2,1,0:T(8,128)(2,1)S(1)} %get-tuple-element.23), channel_id=1, source_target_pairs={{0,4},{4,8},{8,12},{12,16},{16,20},{20,24},{24,28},{1,5},{5,9},{9,... | collective-permute-start | bytes 3145736 | tf_op jit(solution)/shard_map/ppermute | solution.py:37
  214.9 106.4 %all-reduce.5.cloned.1.call-start = ((), (), s32[]{:S(2)}) async-start(), calls=%async_computation | async-start | bytes 262144 | tf_op jit(solution)/shard_map/psum | solution.py:10
  216.6 30.9 %collective-permute-start.8 = (f32[2,64,128]{2,1,0:T(8,128)}, f32[2,64,128]{2,1,0:T(8,128)}, u32[]{:S(2)}, u32[]{:S(2)}) collective-permute-start(f32[2,64,128]{2,1,0:T(8,128)} %add.95), channel_id=1, source_target_pairs={{0,8},{4,12},{8,0},{12,4},{16,24},{20,28},{24,16},{28,20},{1,9},{5... | collective-permute-start | bytes 196616 | tf_op jit(solution)/shard_map/ppermute | solution.py:14
  248.4 5.2 %collective-permute-start.9 = (f32[2,64,128]{2,1,0:T(8,128)S(1)}, f32[2,64,128]{2,1,0:T(8,128)S(1)}, u32[]{:S(2)}, u32[]{:S(2)}) collective-permute-start(f32[2,64,128]{2,1,0:T(8,128)S(1)} %add.97), channel_id=1, source_target_pairs={{0,16},{4,20},{8,24},{12,28},{16,0},{20,4},{24,8},{28,12},{1,17},{... | collective-permute-start | bytes 196616 | tf_op jit(solution)/shard_map/ppermute | solution.py:14
  261.0 2.8 copy-start.1
Sparse Core Ops, SparseCore 0:
  215.0 32.4 all-reduce.6
  251.3 69.8 all-reduce.4
